TPU v7x, 32 devices: a whole 2x2x4 slice. The times are simulated.
32 devices in a mesh: tm: 8 (over z, y), cal: 4 (over x, core).
Axes of the slice: x: 2, y: 2, z: 4, core: 2. Of those that a mesh axis runs over, the one named last changes fastest.
Arguments:
- src_design: float32 [5, 4096, 128], P(None, ('tm', 'cal')), may hold values from -6 to 6
- att_design: float32 [3, 4096, 128], P(None, ('tm', 'cal')), may hold values from -6 to 6
- obs_phase: float32 [4096, 128], P(('tm', 'cal')), may hold values from 0 to 1
- cal_design: float32 [4096, 128], P(('tm', 'cal')), may hold values from -6 to 6
- obs_weight: float32 [4096, 128], P(('tm', 'cal')), may hold values from 0.1 to 12
- knot_index: int32 [4096, 128], P(('tm', 'cal')), may hold values from 0 to 4092, as said below
- cal_block: int32 [4096, 128], P(('tm', 'cal')), may hold values from 0 to 7
- cal_column: int32 [4096, 128], P(('tm', 'cal')), may hold values from 0 to 4095
- obs_count: int32 [4096], P(('tm', 'cal')), may hold values from 32 to 128
- src_res: float32 [5, 4096], P(None, ('tm', 'cal')), may hold values from -6 to 6
- att_res: float32 [3, 4096], P(None, ('tm', 'cal')), may hold values from -6 to 6
- cal_res: float32 [8, 4096], P('cal'), may hold values from -6 to 6
- src_dir: float32 [5, 4096], P(None, ('tm', 'cal')), may hold values from -6 to 6
- att_dir: float32 [3, 4096], P(None, ('tm', 'cal')), may hold values from -6 to 6
- cal_dir: float32 [8, 4096], P('cal'), may hold values from -6 to 6
Outputs:
- new_src_res: float32 [5, 4096], P(None, ('tm', 'cal'))
- new_att_res: float32 [3, 4096], P(None, ('tm', 'cal'))
- new_cal_res: float32 [8, 4096], P('cal')
- new_src_dir: float32 [5, 4096], P(None, ('tm', 'cal'))
- new_att_dir: float32 [3, 4096], P(None, ('tm', 'cal'))
- new_cal_dir: float32 [8, 4096], P('cal')
Inputs may be any that keep to these rules, and one draw needn't show every extreme that they name: The observations of source row s have knot intervals from (s // 128) * 128 to (s // 128) * 128 + 127, and knot_index + 3 < 4096.
All inputs are finite; a program needn't handle non-finite values.
Results may differ from a plain program's by a relative error of at most 0.00015.
Values sent between devices are 32-bit elements; how exact they have to be, the bound alone decides.
No kernel may reach another device: no remote copies, remote signals or barrier semaphores. Data moves between devices by JAX's collectives and lax.ppermute only.
A program may use at most 64 MiB of HBM per device.

v0:
```python
import jax
import jax.numpy as jnp
from jax import lax
from jax.sharding import PartitionSpec as P

EXACT = lax.Precision.HIGHEST


def passed_along(block, axis, distance):
    devices = range(lax.axis_size(axis))
    route = [(i - distance, i) for i in devices if i - distance in devices]
    return lax.ppermute(block, axis, route)


def spline(phase):
    rest = 1.0 - phase
    cube = phase * phase * phase
    square = phase * phase
    first = rest * rest * rest / 6.0
    second = (3.0 * cube - 6.0 * square + 4.0) / 6.0
    third = (-3.0 * cube + 3.0 * square + 3.0 * phase + 1.0) / 6.0
    fourth = cube / 6.0
    return (first, second, third, fourth)


def local(
    src_design,
    att_design,
    obs_phase,
    cal_design,
    obs_weight,
    knot_index,
    cal_block,
    cal_column,
    obs_count,
    src_res,
    att_res,
    cal_res,
    src_dir,
    att_dir,
    cal_dir,
):
    knot_count = att_dir.shape[1]
    blocks, col_width = cal_dir.shape
    all_blocks = blocks * lax.axis_size("cal")
    cal_size = all_blocks * col_width
    lane = 128
    rows = cal_size // lane
    src_rows, slots = obs_phase.shape
    first_row = (lax.axis_index("tm") == 0).astype(jnp.float32)
    cal_values = lax.all_gather(cal_dir, "cal", axis=0, tiled=True)
    edge_knots = passed_along(att_dir[:, :3], ("tm", "cal"), -1)
    att_ext = jnp.concatenate([att_dir, edge_knots], axis=1)
    live_mask = (lax.broadcasted_iota(jnp.int32, obs_phase.shape, 1) < obs_count[:, None]).astype(
        jnp.float32
    )
    basis = spline(obs_phase)
    local_knot = knot_index - lax.axis_index(("tm", "cal")) * knot_count
    knot_iota = lax.broadcasted_iota(jnp.int32, (knot_count, 1, 1), 0)
    knot_hot = (local_knot[None] == knot_iota).astype(jnp.float32)
    table = jnp.stack([att_ext[:, m : m + knot_count].T for m in range(4)], axis=1)
    table = table.reshape(knot_count, 12)
    picked = jnp.einsum("jq,jso->qso", table, knot_hot, precision=EXACT).reshape(
        4, 3, src_rows, slots
    )
    y_att = jnp.zeros_like(obs_phase)
    for m in range(4):
        y_att = y_att + basis[m] * jnp.sum(att_design * picked[m], axis=0)
    flat_index = cal_block * col_width + cal_column
    high = flat_index // lane
    low = flat_index % lane
    high_hot = (high[None] == lax.broadcasted_iota(jnp.int32, (rows, 1, 1), 0)).astype(jnp.float32)
    low_hot = (low[None] == lax.broadcasted_iota(jnp.int32, (lane, 1, 1), 0)).astype(jnp.float32)
    cal_table = cal_values.reshape(rows, lane)
    row_vals = jnp.einsum("hl,hso->lso", cal_table, high_hot, precision=EXACT)
    y_cal = cal_design * jnp.sum(row_vals * low_hot, axis=0)
    y_src = jnp.sum(src_design * src_dir[:, :, None], axis=0)
    response = live_mask * (y_src + y_att + y_cal)
    weighted = obs_weight * response
    curv_local = jnp.sum(weighted * response)
    norm_local = (
        jnp.sum(src_res * src_res)
        + jnp.sum(att_res * att_res)
        + first_row * jnp.sum(cal_res * cal_res)
    )
    q_src = jnp.sum(src_design * weighted[None], axis=2)
    scaled = att_design * weighted[None]
    spread = jnp.stack([basis[m][None] * scaled for m in range(4)], axis=0).reshape(
        12, src_rows, slots
    )
    gathered = jnp.einsum("qso,jso->jq", spread, knot_hot, precision=EXACT).reshape(
        knot_count, 4, 3
    )
    grad_ext = jnp.zeros((3, knot_count + 3), jnp.float32)
    for m in range(4):
        grad_ext = grad_ext + jnp.pad(gathered[:, m, :].T, ((0, 0), (m, 3 - m)))
    incoming = passed_along(grad_ext[:, knot_count:], ("tm", "cal"), 1)
    q_att = jnp.concatenate([grad_ext[:, :3] + incoming, grad_ext[:, 3:knot_count]], axis=1)
    cal_weighted = (cal_design * weighted)[None] * low_hot
    cal_term = jnp.einsum("hso,lso->hl", high_hot, cal_weighted, precision=EXACT)
    scalars = jnp.zeros((1, lane), jnp.float32).at[0, 0].set(norm_local).at[0, 1].set(curv_local)
    packed = jnp.concatenate([cal_term, scalars], axis=0)
    summed = lax.psum(packed, ("tm", "cal"))
    norm_now = summed[rows, 0]
    curvature = summed[rows, 1]
    own = lax.axis_index("cal") * (blocks * col_width // lane)
    q_cal = lax.dynamic_slice_in_dim(summed, own, blocks * col_width // lane, 0).reshape(
        blocks, col_width
    )
    step_len = norm_now / curvature
    new_src_res = src_res - step_len * q_src
    new_att_res = att_res - step_len * q_att
    new_cal_res = cal_res - step_len * q_cal
    next_local = (
        jnp.sum(new_src_res * new_src_res)
        + jnp.sum(new_att_res * new_att_res)
        + first_row * jnp.sum(new_cal_res * new_cal_res)
    )
    norm_next = lax.psum(jnp.zeros((1, lane), jnp.float32).at[0, 0].set(next_local), ("tm", "cal"))[
        0, 0
    ]
    ratio = norm_next / norm_now
    return (
        new_src_res,
        new_att_res,
        new_cal_res,
        new_src_res + ratio * src_dir,
        new_att_res + ratio * att_dir,
        new_cal_res + ratio * cal_dir,
    )


def solution(mesh):
    return jax.shard_map(
        local,
        mesh=mesh,
        in_specs=(
            P(None, ("tm", "cal"), None),
            P(None, ("tm", "cal"), None),
            P(("tm", "cal"), None),
            P(("tm", "cal"), None),
            P(("tm", "cal"), None),
            P(("tm", "cal"), None),
            P(("tm", "cal"), None),
            P(("tm", "cal"), None),
            P(("tm", "cal")),
            P(None, ("tm", "cal")),
            P(None, ("tm", "cal")),
            P("cal", None),
            P(None, ("tm", "cal")),
            P(None, ("tm", "cal")),
            P("cal", None),
        ),
        out_specs=(
            P(None, ("tm", "cal")),
            P(None, ("tm", "cal")),
            P("cal", None),
            P(None, ("tm", "cal")),
            P(None, ("tm", "cal")),
            P("cal", None),
        ),
        check_vma=False,
    )
```

profile of v0, /device:TPU:0, one launch (start us, length us, event | category | flops | bytes accessed | tf_op | source)
XLA Modules:
  0.0 323.5 jit_solution(16515309153429786869)
XLA Ops:
  7.2 1.3 collective-permute-start
  8.5 0.6 compare_reduce_fusion.1
  9.2 0.6 compare_reduce_fusion
  9.8 0.7 constant_dynamic-update-slice_fusion.1
  10.5 1.4 multiply_reduce_fusion.4
  11.9 1.3 multiply_reduce_fusion.8
  13.2 1.3 multiply_reduce_fusion.6
  17.1 0.6 slice.117
  17.7 0.8 broadcast_subtract_fusion
  18.5 0.1 copy.49
  18.6 7.7 %all-gather = f32[4,2,4096]{2,1,0:T(2,128)S(1)} all-gather(f32[1,2,4096]{2,1,0:T(2,128)} %bitcast.78), channel_id=1, replica_groups=mesh['tm'=8,'cal'=4] {'cal'}, dimensions={0}, use_global_device_ids=true | all-gather | bytes 163840 | tf_op jit(solution)/shard_map/all_gather | solution.py:51
  26.2 0.1 reshape.140
  26.4 0.9 add_select_fusion.1
  27.3 0.1 copy.48
  27.4 1.3 iota_compare_fusion.1
  28.7 38.5 %copy.50 = pred[128,128,128]{2,0,1:T(32,128)(4,1)S(1)} copy(pred[128,128,128]{1,0,2:T(32,128)(4,1)S(1)} %iota_compare_fusion.1) | data formatting | bytes 4194304 | tf_op jit(solution)/shard_map/eq | solution.py:60
  67.2 2.7 iota_compare_fusion
  70.0 20.5 %copy.55 = pred[256,128,128]{2,0,1:T(32,128)(4,1)} copy(pred[256,128,128]{1,0,2:T(32,128)(4,1)S(1)} %iota_compare_fusion) | data formatting | bytes 8388608 | tf_op jit(solution)/shard_map/eq | solution.py:72
  90.5 0.1 multiply_reduce_fusion.1
  90.7 8.2 %fusion = f32[128,128]{1,0:T(8,128)S(1)} fusion(s32[128,128]{1,0:T(8,128)S(1)} %get-tuple-element.62, pred[256,128,128]{2,0,1:T(32,128)(4,1)} %copy.55, f32[256,128]{1,0:T(8,128)S(1)} %reshape.140), kind=kOutput, calls=%fused_computation.2 | convolution fusion | flops 6448726016 | bytes 4456448 | tf_op jit(solution)/shard_map/hl,hso->lso/dot_general | solution.py:75
  99.0 0.1 slice_bitcast_fusion.2
  99.1 2.2 fusion.29
  101.3 0.8 fusion.7
  102.2 0.1 fusion.25
  102.3 0.2 multiply_reduce_fusion
  102.4 0.1 multiply_bitcast_fusion.3
  102.6 0.3 copy.59
  102.9 4.2 %fusion.4 = f32[128,4,3]{0,1,2:T(4,128)S(1)} fusion(f32[4,3,128,128]{3,0,2,1:T(4,128)S(1)} %copy.59, s32[128,128]{0,1:T(8,128)S(1)} %copy.49), kind=kOutput, calls=%fused_computation.9 | convolution fusion | flops 304087040 | bytes 858112 | tf_op jit(solution)/shard_map/qso,jso->jq/dot_general | solution.py:91
  107.1 0.1 pad_add_fusion
  107.2 0.1 slice.143
  107.3 0.6 multiply_reduce_fusion.2
  107.9 2.2 collective-permute-start.1
  110.1 4.7 %fusion.1 = f32[128,128,128]{2,0,1:T(8,128)} fusion(f32[128,128]{1,0:T(8,128)S(1)} %get-tuple-element.52, s32[128,128]{1,0:T(8,128)S(1)} %get-tuple-element.62), kind=kLoop, calls=%fused_computation.5 | loop fusion | flops 4194304 | bytes 8519680 | tf_op jit(solution)/shard_map/mul | solution.py:99
  114.8 9.3 %copy.57 = f32[128,128,128]{1,0,2:T(8,128)} copy(f32[128,128,128]{2,0,1:T(8,128)} %fusion.1) | data formatting | bytes 16777216 | tf_op jit(solution)/shard_map/mul | solution.py:99
  124.2 11.2 %convolution_bitcast_fusion = f32[256,128]{1,0:T(8,128)S(1)} fusion(f32[128,128,128]{1,0,2:T(8,128)} %copy.57, s32[128,128]{0,1:T(8,128)S(1)} %copy.48), kind=kOutput, calls=%fused_computation.8 | convolution fusion | flops 6446645248 | bytes 8585216 | tf_op jit(solution)/shard_map/hso,lso->hl/dot_general | solution.py:100
  135.3 2.5 fusion.28
  137.9 1.4 scatter.11
  139.3 0.7 pad_maximum_fusion
  140.0 123.3 %all-reduce.8.cloned.1.call-done = f32[257,128]{1,0:T(8,128)} async-done(((f32[257,128]{1,0:T(8,128)}), f32[257,128]{1,0:T(8,128)}) %all-reduce.8.cloned.1.call-update) | async-done | bytes 131600 | tf_op jit(solution)/shard_map/psum | solution.py:103
  263.3 1.3 fusion.26
  266.0 0.8 dynamic-slice_multiply_fusion
  266.8 0.6 multiply_reduce_fusion.5
  267.4 0.7 multiply_reduce_fusion.3
  268.8 0.8 multiply_reduce_fusion.7
  271.6 42.5 %psum.15 = f32[1,128]{1,0:T(1,128)S(1)} all-reduce(f32[1,128]{1,0:T(1,128)S(1)} %scatter.14), channel_id=1, replica_groups=mesh['tm'=8,'cal'=4] {'tm','cal'}, use_global_device_ids=true, to_apply=%region_17.18 | all-reduce | flops 128 | bytes 1024 | tf_op jit(solution)/shard_map/psum | solution.py:119
  314.8 0.6 multiply_add_fusion.3
  315.4 0.6 multiply_add_fusion.2
  316.0 0.6 multiply_add_fusion.1
  (47 shorter events, 0.3 us)
Async XLA Ops:
  7.2 256.2 %all-reduce.8.cloned.1.call-start = ((), (), s32[]{:S(2)}) async-start(), calls=%async_computation | async-start | bytes 270336 | tf_op jit(solution)/shard_map/psum | solution.py:103
  7.2 91.8 %collective-permute-start = (f32[3,3]{1,0:T(4,128)}, f32[3,3]{1,0:T(4,128)S(1)}, u32[]{:S(2)}, u32[]{:S(2)}) collective-permute-start(f32[3,3]{1,0:T(4,128)} %bitcast.79), channel_id=1, source_target_pairs={{1,0},{2,1},{3,2},{4,3},{5,4},{6,5},{7,6},{8,7},{9,8},{10,9},{11,1... | collective-permute-start | bytes 116 | tf_op jit(solution)/shard_map/ppermute | solution.py:12
  69.9 20.6 %copy-start = (f32[5,128,128]{2,1,0:T(8,128)S(1)}, f32[5,128,128]{2,1,0:T(8,128)}, u32[]{:S(2)}) copy-start(f32[5,128,128]{2,1,0:T(8,128)} %param.21) | copy-start | bytes 983044
  69.9 20.6 %copy-start.9 = (f32[5,128]{1,0:T(8,128)S(1)}, f32[5,128]{1,0:T(8,128)}, u32[]{:S(2)}) copy-start(f32[5,128]{1,0:T(8,128)} %param.33) | copy-start | bytes 7684
  90.7 8.4 %copy-start.8 = (f32[3,128]{1,0:T(4,128)S(1)}, f32[3,128]{1,0:T(4,128)}, u32[]{:S(2)}) copy-start(f32[3,128]{1,0:T(4,128)} %param.34) | copy-start | bytes 4612
  90.7 10.6 %copy-start.1 = (f32[3,128,128]{2,1,0:T(8,128)S(1)}, f32[3,128,128]{2,1,0:T(8,128)}, u32[]{:S(2)}) copy-start(f32[3,128,128]{2,1,0:T(8,128)} %param.22) | copy-start | bytes 589828
  98.9 3.2 copy-start.5
  98.9 3.2 copy-start.6
  98.9 3.2 copy-start.7
  99.0 3.2 copy-start.14
  107.9 32.1 %collective-permute-start.1 = (f32[3,3]{1,0:T(4,128)S(1)}, f32[3,3]{1,0:T(4,128)S(1)}, u32[]{:S(2)}, u32[]{:S(2)}) collective-permute-start(f32[3,3]{1,0:T(4,128)S(1)} %slice.142), channel_id=1, source_target_pairs={{0,1},{1,2},{2,3},{3,4},{4,5},{5,6},{6,7},{7,8},{8,9},{9,10},{10,1... | collective-permute-start | bytes 116 | tf_op jit(solution)/shard_map/ppermute | solution.py:12
  124.2 142.6 %copy-start.11 = (f32[5,128]{1,0:T(8,128)S(1)}, f32[5,128]{1,0:T(8,128)}, u32[]{:S(2)}) copy-start(f32[5,128]{1,0:T(8,128)} %param.30) | copy-start | bytes 7684
  124.2 143.3 %copy-start.4 = (f32[2,4096]{1,0:T(2,128)S(1)}, f32[2,4096]{1,0:T(2,128)}, u32[]{:S(2)}) copy-start(f32[2,4096]{1,0:T(2,128)} %param.32) | copy-start | bytes 98308
  124.2 144.7 %copy-start.12 = (f32[3,128]{1,0:T(4,128)S(1)}, f32[3,128]{1,0:T(4,128)}, u32[]{:S(2)}) copy-start(f32[3,128]{1,0:T(4,128)} %param.31) | copy-start | bytes 4612
  124.2 191.8 %copy-start.2 = (f32[2,4096]{1,0:T(2,128)S(1)}, f32[2,4096]{1,0:T(2,128)}, u32[]{:S(2)}) copy-start(f32[2,4096]{1,0:T(2,128)} %param.35) | copy-start | bytes 98308
  267.4 49.2 %copy-start.10 = (f32[5,128]{1,0:T(8,128)}, f32[5,128]{1,0:T(8,128)S(1)}, u32[]{:S(2)}) copy-start(f32[5,128]{1,0:T(8,128)S(1)} %get-tuple-element.51) | copy-start | bytes 7684
  268.1 48.5 %copy-start.3 = (f32[2,4096]{1,0:T(2,128)}, f32[2,4096]{1,0:T(2,128)S(1)}, u32[]{:S(2)}) copy-start(f32[2,4096]{1,0:T(2,128)S(1)} %get-tuple-element.47) | copy-start | bytes 98308
  269.6 47.1 %copy-start.13 = (f32[3,128]{1,0:T(4,128)}, f32[3,128]{1,0:T(4,128)S(1)}, u32[]{:S(2)}) copy-start(f32[3,128]{1,0:T(4,128)S(1)} %get-tuple-element.49) | copy-start | bytes 4612
Sparse Core Ops, SparseCore 0:
  140.1 123.1 all-reduce.7
where the time goes:
time: 324 us
  waiting for transfers between devices  123 us (38%)
  local copies, waits for them, and re-layouts  73.3 us (23%)
  blocking collectives  50.1 us (15%)
  matrix products  25.8 us (8%)
  other arithmetic  25.7 us (8%)
  between operations  21.7 us (7%)
  starting transfers between devices  3.56 us (1%)
    psum x1, waiting for transfers between devices, local(): summed = lax.psum(packed, ('tm', 'cal'))  123 us
    psum x1, blocking collectives, local(): lax.psum(jnp.zeros((1, lane), jnp.float32).at[0, 0].set(next_local), ('tm...  42.5 us
    eq x1, local copies, waits for them, and re-layouts, local(): knot_hot = (local_knot[None] == knot_iota).astype(jnp.float32)  38.5 us
    eq x1, local copies, waits for them, and re-layouts, local(): high[None] == lax.broadcasted_iota(jnp.int32, (rows, 1, 1), 0)  20.5 us
    dot_general x1, matrix products, local(): jnp.einsum('hso,lso->hl', high_hot, cal_weighted, precision=EXACT)  11.2 us
    mul x1, local copies, waits for them, and re-layouts, local(): cal_weighted = (cal_design * weighted)[None] * low_hot  9.32 us
    dot_general x1, matrix products, local(): row_vals = jnp.einsum('hl,hso->lso', cal_table, high_hot, precision=EXACT)  8.23 us
    all_gather x1, blocking collectives, local(): cal_values = lax.all_gather(cal_dir, 'cal', axis=0, tiled=True)  7.65 us
  transfers between devices with their start and end apart: 3, of which 1 were waited for; matrix products, arithmetic and copies ran while one was open for 34% of the time, Pallas kernels for 0%

commit v1 on v0

--- a/solution.py
+++ b/solution.py
@@ -100,7 +100,7 @@
     cal_term = jnp.einsum("hso,lso->hl", high_hot, cal_weighted, precision=EXACT)
     scalars = jnp.zeros((1, lane), jnp.float32).at[0, 0].set(norm_local).at[0, 1].set(curv_local)
     packed = jnp.concatenate([cal_term, scalars], axis=0)
-    summed = lax.psum(packed, ("tm", "cal"))
+    summed = lax.psum(lax.psum(packed, "cal"), "tm")
     norm_now = summed[rows, 0]
     curvature = summed[rows, 1]
     own = lax.axis_index("cal") * (blocks * col_width // lane)

time: 324 us -> 306 us (0.944)
  waiting for transfers between devices: 123 us -> 108 us
    psum x1 -> x2, waiting for transfers between devices: 123 us -> 108 us  [local(): summed = lax.psum(lax.psum(packed, 'cal'), 'tm')]
  transfers between devices with their start and end apart: 3 -> 4, of which waited for: 1 -> 2; matrix products, arithmetic and copies ran while one was open for 34% -> 36% of each run, Pallas kernels for 0% -> 0%
where the time goes in v1:
time: 306 us; the launch traced here: 305 us
  waiting for transfers between devices  108 us (35%)
  local copies, waits for them, and re-layouts  73.3 us (24%)
  blocking collectives  47.2 us (15%)
  matrix products  25.8 us (8%)
  other arithmetic  25.7 us (8%)
  between operations  21.7 us (7%)
  starting transfers between devices  3.6 us (1%)
    psum x2, waiting for transfers between devices, local(): summed = lax.psum(lax.psum(packed, 'cal'), 'tm')  108 us
    psum x1, blocking collectives, local(): lax.psum(jnp.zeros((1, lane), jnp.float32).at[0, 0].set(next_local), ('tm...  39.6 us
    eq x1, local copies, waits for them, and re-layouts, local(): knot_hot = (local_knot[None] == knot_iota).astype(jnp.float32)  38.5 us
    eq x1, local copies, waits for them, and re-layouts, local(): high[None] == lax.broadcasted_iota(jnp.int32, (rows, 1, 1), 0)  20.5 us
    dot_general x1, matrix products, local(): jnp.einsum('hso,lso->hl', high_hot, cal_weighted, precision=EXACT)  11.2 us
    mul x1, local copies, waits for them, and re-layouts, local(): cal_weighted = (cal_design * weighted)[None] * low_hot  9.32 us
    dot_general x1, matrix products, local(): row_vals = jnp.einsum('hl,hso->lso', cal_table, high_hot, precision=EXACT)  8.23 us
    all_gather x1, blocking collectives, local(): cal_values = lax.all_gather(cal_dir, 'cal', axis=0, tiled=True)  7.65 us
  transfers between devices with their start and end apart: 4, of which 2 were waited for; matrix products, arithmetic and copies ran while one was open for 36% of the time, Pallas kernels for 0%

profile of v1, /device:TPU:0, one launch (start us, length us, event | category | flops | bytes accessed | tf_op | source)
XLA Modules:
  0.0 305.1 jit_solution(16554708595357695252)
XLA Ops:
  7.2 1.3 collective-permute-start
  8.5 0.6 compare_reduce_fusion.1
  9.2 0.6 compare_reduce_fusion
  9.8 0.7 constant_dynamic-update-slice_fusion.1
  10.5 1.4 multiply_reduce_fusion.4
  11.9 1.3 multiply_reduce_fusion.8
  13.2 1.3 multiply_reduce_fusion.6
  17.1 0.6 slice.117
  17.7 0.8 broadcast_subtract_fusion
  18.5 0.1 copy.49
  18.6 7.7 %all-gather = f32[4,2,4096]{2,1,0:T(2,128)S(1)} all-gather(f32[1,2,4096]{2,1,0:T(2,128)} %bitcast.78), channel_id=1, replica_groups=mesh['tm'=8,'cal'=4] {'cal'}, dimensions={0}, use_global_device_ids=true | all-gather | bytes 163840 | tf_op jit(solution)/shard_map/all_gather | solution.py:51
  26.2 0.1 reshape.140
  26.4 0.9 add_select_fusion.1
  27.3 0.1 copy.48
  27.4 1.3 iota_compare_fusion.1
  28.7 38.5 %copy.50 = pred[128,128,128]{2,0,1:T(32,128)(4,1)S(1)} copy(pred[128,128,128]{1,0,2:T(32,128)(4,1)S(1)} %iota_compare_fusion.1) | data formatting | bytes 4194304 | tf_op jit(solution)/shard_map/eq | solution.py:60
  67.2 2.7 iota_compare_fusion
  69.9 20.5 %copy.55 = pred[256,128,128]{2,0,1:T(32,128)(4,1)} copy(pred[256,128,128]{1,0,2:T(32,128)(4,1)S(1)} %iota_compare_fusion) | data formatting | bytes 8388608 | tf_op jit(solution)/shard_map/eq | solution.py:72
  90.5 0.1 multiply_reduce_fusion.1
  90.7 8.2 %fusion = f32[128,128]{1,0:T(8,128)S(1)} fusion(s32[128,128]{1,0:T(8,128)S(1)} %get-tuple-element.62, pred[256,128,128]{2,0,1:T(32,128)(4,1)} %copy.55, f32[256,128]{1,0:T(8,128)S(1)} %reshape.140), kind=kOutput, calls=%fused_computation.2 | convolution fusion | flops 6448726016 | bytes 4456448 | tf_op jit(solution)/shard_map/hl,hso->lso/dot_general | solution.py:75
  99.0 0.1 slice_bitcast_fusion.2
  99.1 2.2 fusion.29
  101.3 0.8 fusion.7
  102.1 0.1 fusion.25
  102.4 0.3 copy.59
  102.7 4.2 %fusion.4 = f32[128,4,3]{0,1,2:T(4,128)S(1)} fusion(f32[4,3,128,128]{3,0,2,1:T(4,128)S(1)} %copy.59, s32[128,128]{0,1:T(8,128)S(1)} %copy.49), kind=kOutput, calls=%fused_computation.9 | convolution fusion | flops 304087040 | bytes 858112 | tf_op jit(solution)/shard_map/qso,jso->jq/dot_general | solution.py:91
  106.9 0.1 pad_add_fusion
  107.0 0.1 slice.143
  107.1 0.6 multiply_reduce_fusion.2
  107.7 2.2 collective-permute-start.1
  109.9 4.7 %fusion.1 = f32[128,128,128]{2,0,1:T(8,128)} fusion(f32[128,128]{1,0:T(8,128)S(1)} %get-tuple-element.52, s32[128,128]{1,0:T(8,128)S(1)} %get-tuple-element.62), kind=kLoop, calls=%fused_computation.5 | loop fusion | flops 4194304 | bytes 8519680 | tf_op jit(solution)/shard_map/mul | solution.py:99
  114.7 9.3 %copy.57 = f32[128,128,128]{1,0,2:T(8,128)} copy(f32[128,128,128]{2,0,1:T(8,128)} %fusion.1) | data formatting | bytes 16777216 | tf_op jit(solution)/shard_map/mul | solution.py:99
  124.0 11.2 %convolution_bitcast_fusion = f32[256,128]{1,0:T(8,128)S(1)} fusion(f32[128,128,128]{1,0,2:T(8,128)} %copy.57, s32[128,128]{0,1:T(8,128)S(1)} %copy.48), kind=kOutput, calls=%fused_computation.8 | convolution fusion | flops 6446645248 | bytes 8585216 | tf_op jit(solution)/shard_map/hso,lso->hl/dot_general | solution.py:100
  135.2 2.5 fusion.28
  137.7 1.4 scatter.11
  139.1 0.7 pad_maximum_fusion
  139.8 0.2 multiply_reduce_fusion
  140.0 32.8 %all-reduce.9.cloned.1.call-done = f32[257,128]{1,0:T(8,128)} async-done(((f32[257,128]{1,0:T(8,128)}), f32[257,128]{1,0:T(8,128)}) %all-reduce.9.cloned.1.call-update) | async-done | bytes 131600 | tf_op jit(solution)/shard_map/psum | solution.py:103
  172.8 75.0 %all-reduce.11.cloned.1.call-done = f32[257,128]{1,0:T(8,128)} async-done(((f32[257,128]{1,0:T(8,128)}), f32[257,128]{1,0:T(8,128)}) %all-reduce.11.cloned.1.call-update) | async-done | bytes 131600 | tf_op jit(solution)/shard_map/psum | solution.py:103
  247.8 1.3 fusion.26
  250.5 0.8 dynamic-slice_multiply_fusion
  251.3 0.6 multiply_reduce_fusion.5
  251.9 0.7 multiply_reduce_fusion.3
  253.4 0.8 multiply_reduce_fusion.7
  256.1 39.6 %psum.23 = f32[1,128]{1,0:T(1,128)S(1)} all-reduce(f32[1,128]{1,0:T(1,128)S(1)} %scatter.14), channel_id=1, replica_groups=mesh['tm'=8,'cal'=4] {'tm','cal'}, use_global_device_ids=true, to_apply=%region_18.19 | all-reduce | flops 128 | bytes 1024 | tf_op jit(solution)/shard_map/psum | solution.py:119
  296.4 0.6 multiply_add_fusion.3
  297.0 0.6 multiply_add_fusion.2
  297.6 0.6 multiply_add_fusion.1
  (50 shorter events, 0.4 us)
Async XLA Ops:
  7.2 165.6 %all-reduce.9.cloned.1.call-start = ((), (), s32[]{:S(2)}) async-start(), calls=%async_computation | async-start | bytes 270336 | tf_op jit(solution)/shard_map/psum | solution.py:103
  7.2 91.8 %collective-permute-start = (f32[3,3]{1,0:T(4,128)}, f32[3,3]{1,0:T(4,128)S(1)}, u32[]{:S(2)}, u32[]{:S(2)}) collective-permute-start(f32[3,3]{1,0:T(4,128)} %bitcast.79), channel_id=1, source_target_pairs={{1,0},{2,1},{3,2},{4,3},{5,4},{6,5},{7,6},{8,7},{9,8},{10,9},{11,1... | collective-permute-start | bytes 116 | tf_op jit(solution)/shard_map/ppermute | solution.py:12
  69.9 20.6 %copy-start = (f32[5,128,128]{2,1,0:T(8,128)S(1)}, f32[5,128,128]{2,1,0:T(8,128)}, u32[]{:S(2)}) copy-start(f32[5,128,128]{2,1,0:T(8,128)} %param.21) | copy-start | bytes 983044
  69.9 20.6 %copy-start.9 = (f32[5,128]{1,0:T(8,128)S(1)}, f32[5,128]{1,0:T(8,128)}, u32[]{:S(2)}) copy-start(f32[5,128]{1,0:T(8,128)} %param.33) | copy-start | bytes 7684
  90.7 8.4 %copy-start.8 = (f32[3,128]{1,0:T(4,128)S(1)}, f32[3,128]{1,0:T(4,128)}, u32[]{:S(2)}) copy-start(f32[3,128]{1,0:T(4,128)} %param.34) | copy-start | bytes 4612
  90.7 10.6 %copy-start.1 = (f32[3,128,128]{2,1,0:T(8,128)S(1)}, f32[3,128,128]{2,1,0:T(8,128)}, u32[]{:S(2)}) copy-start(f32[3,128,128]{2,1,0:T(8,128)} %param.22) | copy-start | bytes 589828
  98.9 3.2 %copy-start.5 = (f32[128,128]{1,0:T(8,128)S(1)}, f32[128,128]{1,0:T(8,128)}, u32[]{:S(2)}) copy-start(f32[128,128]{1,0:T(8,128)} %param.24) | copy-start | bytes 196612
  98.9 3.2 %copy-start.6 = (f32[128,128]{1,0:T(8,128)S(1)}, f32[128,128]{1,0:T(8,128)}, u32[]{:S(2)}) copy-start(f32[128,128]{1,0:T(8,128)} %param.25) | copy-start | bytes 196612
  98.9 3.2 %copy-start.7 = (f32[128,128]{1,0:T(8,128)S(1)}, f32[128,128]{1,0:T(8,128)}, u32[]{:S(2)}) copy-start(f32[128,128]{1,0:T(8,128)} %param.23) | copy-start | bytes 196612
  99.0 3.2 %copy-start.14 = (s32[128]{0:T(128)S(1)}, s32[128]{0:T(128)}, u32[]{:S(2)}) copy-start(s32[128]{0:T(128)} %param.29) | copy-start | bytes 1540
  107.7 65.1 %collective-permute-start.1 = (f32[3,3]{1,0:T(4,128)S(1)}, f32[3,3]{1,0:T(4,128)S(1)}, u32[]{:S(2)}, u32[]{:S(2)}) collective-permute-start(f32[3,3]{1,0:T(4,128)S(1)} %slice.142), channel_id=1, source_target_pairs={{0,1},{1,2},{2,3},{3,4},{4,5},{5,6},{6,7},{7,8},{8,9},{9,10},{10,1... | collective-permute-start | bytes 116 | tf_op jit(solution)/shard_map/ppermute | solution.py:12
  124.0 127.3 %copy-start.11 = (f32[5,128]{1,0:T(8,128)S(1)}, f32[5,128]{1,0:T(8,128)}, u32[]{:S(2)}) copy-start(f32[5,128]{1,0:T(8,128)} %param.30) | copy-start | bytes 7684
  124.0 128.0 %copy-start.4 = (f32[2,4096]{1,0:T(2,128)S(1)}, f32[2,4096]{1,0:T(2,128)}, u32[]{:S(2)}) copy-start(f32[2,4096]{1,0:T(2,128)} %param.32) | copy-start | bytes 98308
  124.0 129.4 %copy-start.12 = (f32[3,128]{1,0:T(4,128)S(1)}, f32[3,128]{1,0:T(4,128)}, u32[]{:S(2)}) copy-start(f32[3,128]{1,0:T(4,128)} %param.31) | copy-start | bytes 4612
  124.0 173.6 %copy-start.2 = (f32[2,4096]{1,0:T(2,128)S(1)}, f32[2,4096]{1,0:T(2,128)}, u32[]{:S(2)}) copy-start(f32[2,4096]{1,0:T(2,128)} %param.35) | copy-start | bytes 98308
  139.8 108.0 %all-reduce.11.cloned.1.call-start = ((), (), s32[]{:S(2)}) async-start(), calls=%async_computation.1 | async-start | bytes 270336 | tf_op jit(solution)/shard_map/psum | solution.py:103
  251.9 46.3 %copy-start.10 = (f32[5,128]{1,0:T(8,128)}, f32[5,128]{1,0:T(8,128)S(1)}, u32[]{:S(2)}) copy-start(f32[5,128]{1,0:T(8,128)S(1)} %get-tuple-element.51) | copy-start | bytes 7684
  252.7 45.6 %copy-start.3 = (f32[2,4096]{1,0:T(2,128)}, f32[2,4096]{1,0:T(2,128)S(1)}, u32[]{:S(2)}) copy-start(f32[2,4096]{1,0:T(2,128)S(1)} %get-tuple-element.47) | copy-start | bytes 98308
  254.1 44.1 %copy-start.13 = (f32[3,128]{1,0:T(4,128)}, f32[3,128]{1,0:T(4,128)S(1)}, u32[]{:S(2)}) copy-start(f32[3,128]{1,0:T(4,128)S(1)} %get-tuple-element.49) | copy-start | bytes 4612
Sparse Core Ops, SparseCore 0:
  139.9 32.8 all-reduce.8
  176.5 71.2 all-reduce.10
